TPU v7x, 256 devices: a whole 4x4x8 slice. The times are simulated.
256 devices in a mesh: ctx: 64 (over y, z, core), head: 4 (over x).
Axes of the slice: x: 4, y: 4, z: 8, core: 2. Of those that a mesh axis runs over, the one named last changes fastest.
Arguments:
- queries: bfloat16 [8192, 4096], P('ctx', 'head'), may hold values from -6 to 6
- key_heads: bfloat16 [8192, 4096], P('ctx', 'head'), may hold values from -0.59765625 to 0.59765625
- value_heads: bfloat16 [8192, 4096], P('ctx', 'head'), may hold values from -12 to 12
- gate_logits: bfloat16 [8192, 4096], P('ctx', 'head'), may hold values from -9 to 9
- log_decay: float32 [8192, 32], P('ctx', 'head'), may hold values from -2 to 0
- attn_gain: float32 [4096], P('head'), may hold values from 0.25 to 1.75
- out_weight: bfloat16 [32, 128, 6144], P('head', 'ctx'), may hold values from -0.09375 to 0.09375
- residual: bfloat16 [8192, 6144], P('ctx'), may hold values from -24 to 24
- norm_gain: float32 [6144], replicated, may hold values from 0.25 to 1.75
- router_weight: bfloat16 [6144, 32], replicated, may hold values from -0.078125 to 0.078125
- expert_ids: int32 [8192, 2], P('ctx'), may hold values from 0 to 31, as said below
- expert_gate: bfloat16 [36864, 6144], P(('ctx', 'head')), may hold values from -0.078125 to 0.078125
- expert_up: bfloat16 [36864, 6144], P(('ctx', 'head')), may hold values from -0.078125 to 0.078125
- expert_down: bfloat16 [36864, 6144], P('ctx', 'head'), may hold values from -0.09375 to 0.09375
Outputs:
- layer_out: bfloat16 [8192, 6144], P('ctx', 'head')
Inputs may be any that keep to these rules, and one draw needn't show every extreme that they name: `expert_ids`: A row's two ids differ; within the 128 rows of one block no id is named by more than 10 rows.
All inputs are finite; a program needn't handle non-finite values.
Results may differ from a plain program's by a relative error of at most 0.008.
Values may be sent and summed in bfloat16 or wider, within the bound.
No kernel may reach another device: no remote copies, remote signals or barrier semaphores. Data moves between devices by JAX's collectives and lax.ppermute only.
A program may use at most 128 MiB of HBM per device.

v0:
```python
import jax
import jax.numpy as jnp
from jax import lax
from jax.sharding import Mesh, PartitionSpec as P

EXP = 8
MOST = 10
CTX = ("g", "q", "core")
epsilon = 1e-06
highest = lax.Precision.HIGHEST


def pack_state(factor, state):
    heads, dim, _ = state.shape
    extra = jnp.broadcast_to(factor[:, None, None], (heads, 8, dim))
    return jnp.concatenate([state, extra], axis=1)


def unpack_state(packed):
    dim = packed.shape[-1]
    return (packed[:, dim, 0], packed[:, :dim, :])


def prefix_scan(factor, state, axis, count):
    place = lax.axis_index(axis)

    def shift(value, distance):
        return lax.ppermute(value, axis, [(i, i + distance) for i in range(count - distance)])

    identity = pack_state(jnp.ones_like(factor), jnp.zeros_like(state))
    current = jnp.where(place >= 1, shift(pack_state(factor, state), 1), identity)
    distance = 1
    while distance < count:
        earlier_factor, earlier_state = unpack_state(shift(current, distance))
        later_factor, later_state = unpack_state(current)
        joined = pack_state(
            earlier_factor * later_factor, later_factor[:, None, None] * earlier_state + later_state
        )
        current = jnp.where(place >= distance, joined, current)
        distance *= 2
    return unpack_state(current)[1]


def body(
    queries,
    key_heads,
    value_heads,
    gate_logits,
    log_decay,
    attn_gain,
    out_weight,
    residual,
    norm_gain,
    router_weight,
    expert_ids,
    expert_gate,
    expert_up,
    expert_down,
):
    ctx_count = lax.axis_size(CTX)
    head_count = lax.axis_size("head")
    head_index = lax.axis_index("head")
    tok_rows = queries.shape[0]
    local_heads = log_decay.shape[1]
    head_dim = queries.shape[1] // local_heads
    model_width = residual.shape[1]
    share_width = model_width // head_count
    query_blocks = queries.reshape(tok_rows, local_heads, head_dim)
    key_blocks = key_heads.reshape(tok_rows, local_heads, head_dim)
    value_blocks = value_heads.reshape(tok_rows, local_heads, head_dim)
    cumulative = jnp.cumsum(log_decay, axis=0)
    block_total = cumulative[-1]
    keys_decayed = (
        key_blocks.astype(jnp.float32) * jnp.exp(block_total[None, :] - cumulative)[:, :, None]
    ).astype(jnp.bfloat16)
    local_state = jnp.einsum(
        "thd,the->hde", keys_decayed, value_blocks, preferred_element_type=jnp.float32
    )
    core = lax.axis_index("core")
    swap = [(0, 1), (1, 0)]
    factor = jnp.exp(block_total)
    partner_factor, partner_state = unpack_state(
        lax.ppermute(pack_state(factor, local_state), "core", swap)
    )
    first_factor = jnp.where(core == 0, factor, partner_factor)
    first_state = jnp.where(core == 0, local_state, partner_state)
    second_factor = jnp.where(core == 0, partner_factor, factor)
    second_state = jnp.where(core == 0, partner_state, local_state)
    chip_factor = first_factor * second_factor
    chip_state = second_factor[:, None, None] * first_state + second_state
    half = local_heads // 2
    half_factor = jnp.where(core == 0, chip_factor[:half], chip_factor[half:])
    half_state = jnp.where(core == 0, chip_state[:half], chip_state[half:])
    mine = prefix_scan(half_factor, half_state, ("g", "q"), ctx_count // 2)
    other = lax.ppermute(mine, "core", swap)
    chip_entering = jnp.concatenate(
        [jnp.where(core == 0, mine, other), jnp.where(core == 0, other, mine)], axis=0
    )
    entering = jnp.where(
        core == 0, chip_entering, first_factor[:, None, None] * chip_entering + first_state
    )
    sequence_offsets = jnp.arange(tok_rows)
    causal = (sequence_offsets[:, None] >= sequence_offsets[None, :])[None, :, :]
    cum_heads = cumulative.T
    decay_gaps = jnp.where(causal, cum_heads[:, :, None] - cum_heads[:, None, :], 0.0)
    scores = jnp.einsum(
        "thd,shd->hts", query_blocks, key_blocks, preferred_element_type=jnp.float32
    )
    attn_probs = jnp.where(causal, scores * jnp.exp(decay_gaps), 0.0).astype(jnp.bfloat16)
    within = jnp.einsum(
        "hts,shd->thd", attn_probs, value_blocks, preferred_element_type=jnp.float32
    )
    carried = jnp.einsum(
        "thd,hde->the", query_blocks.astype(jnp.float32), entering, precision=highest
    )
    attended = within + carried * jnp.exp(cumulative)[:, :, None]
    rms_scale = lax.rsqrt(jnp.mean(attended * attended, axis=-1, keepdims=True) + epsilon)
    gate_open = jax.nn.sigmoid(
        gate_logits.astype(jnp.float32).reshape(tok_rows, local_heads, head_dim)
    )
    attn_mixed = (
        attended * rms_scale * attn_gain.reshape(local_heads, head_dim) * gate_open
    ).astype(jnp.bfloat16)
    half_width = share_width // 2
    split_weight = out_weight.reshape(local_heads, -1, head_count, 2, half_width)
    mine = jnp.where(core == 0, split_weight[:, :, :, 0], split_weight[:, :, :, 1])
    theirs = jnp.where(core == 0, split_weight[:, :, :, 1], split_weight[:, :, :, 0])
    received = lax.ppermute(theirs, "core", swap)
    pair_rows = jnp.concatenate(
        [jnp.where(core == 0, mine, received), jnp.where(core == 0, received, mine)], axis=1
    )
    row_whole = lax.all_gather(pair_rows, ("g", "q"), axis=1, tiled=True)
    partner_mixed = lax.ppermute(attn_mixed, "core", swap)
    both_mixed = jnp.concatenate(
        [
            jnp.where(core == 0, attn_mixed, partner_mixed),
            jnp.where(core == 0, partner_mixed, attn_mixed),
        ],
        axis=0,
    )
    partial_sum = jnp.einsum(
        "thr,hrqd->tqd", both_mixed, row_whole, preferred_element_type=jnp.float32
    )
    scattered = lax.psum_scatter(
        partial_sum.astype(jnp.bfloat16), "head", scatter_dimension=1, tiled=True
    ).reshape(2, tok_rows, half_width)
    own_rows = jnp.where(core == 0, scattered[0], scattered[1])
    other_rows = lax.ppermute(jnp.where(core == 0, scattered[1], scattered[0]), "core", swap)
    projected = jnp.concatenate(
        [jnp.where(core == 0, own_rows, other_rows), jnp.where(core == 0, other_rows, own_rows)],
        axis=1,
    ).astype(jnp.float32)
    share_start = head_index * share_width
    residual_share = lax.dynamic_slice_in_dim(residual, share_start, share_width, 1)
    gain_share = lax.dynamic_slice_in_dim(norm_gain, share_start, share_width, 0)
    router_share = lax.dynamic_slice_in_dim(router_weight, share_start, share_width, 0)
    hidden_share = residual_share.astype(jnp.float32) + projected
    router_part = jnp.dot(
        hidden_share * gain_share[None, :], router_share.astype(jnp.float32), precision=highest
    )
    square_part = jnp.sum(hidden_share * hidden_share, axis=-1, keepdims=True)
    stats = lax.psum(jnp.concatenate([square_part, router_part], axis=1), "head")
    row_scale = lax.rsqrt(stats[:, :1] / model_width + epsilon)
    logits = stats[:, 1:] * row_scale
    normed_share = (hidden_share * row_scale * gain_share[None, :]).astype(jnp.bfloat16)
    columns = jnp.arange(router_weight.shape[1], dtype=jnp.int32)
    picked = jnp.sum(
        jnp.where(columns[None, None, :] == expert_ids[:, :, None], logits[:, None, :], 0.0),
        axis=-1,
    )
    route_gates = jax.nn.sigmoid(picked - picked[:, ::-1])
    route_ids = expert_ids.reshape(-1)
    onehot = (route_ids[:, None] == jnp.arange(EXP, dtype=jnp.int32)[None, :]).astype(jnp.int32)
    before_count = jnp.cumsum(onehot, axis=0) - onehot
    slot_index = jnp.sum(before_count * onehot, axis=1)
    slot_range = jnp.arange(MOST, dtype=jnp.int32)
    placed = (onehot.T[:, None, :] == 1) & (slot_index[None, None, :] == slot_range[None, :, None])
    chooser = (
        jnp.sum(placed.reshape(EXP, MOST, tok_rows, 2).astype(jnp.float32), axis=3)
        .astype(jnp.bfloat16)
        .reshape(EXP * MOST, tok_rows)
    )
    weighted = jnp.sum(
        (placed.astype(jnp.float32) * route_gates.reshape(-1)[None, None, :]).reshape(
            EXP, MOST, tok_rows, 2
        ),
        axis=3,
    )
    group = ctx_count // EXP
    packed = (
        jnp.dot(chooser, normed_share, preferred_element_type=jnp.float32)
        .astype(jnp.bfloat16)
        .reshape(EXP, MOST, share_width)
    )
    by_group = lax.all_to_all(packed, "g", split_axis=0, concat_axis=0, tiled=True)
    wide = lax.all_gather(by_group.reshape(EXP * MOST, share_width), "head", axis=1, tiled=True)
    own_parity = lax.all_gather(wide, "q", axis=0, tiled=False)
    other_parity = lax.ppermute(own_parity, "core", swap)
    pairs = group // 2
    halves = []
    for part in (own_parity, other_parity):
        part_rows = part.reshape(-1, model_width)
        gate_part = jnp.einsum(
            "rd,fd->rf", part_rows, expert_gate, preferred_element_type=jnp.float32
        )
        up_part = jnp.einsum("rd,fd->rf", part_rows, expert_up, preferred_element_type=jnp.float32)
        halves.append((jax.nn.silu(gate_part) * up_part).astype(jnp.bfloat16))
    hidden_units = jnp.concatenate(halves, axis=0)
    joined = lax.all_gather(hidden_units, "head", axis=1, tiled=True)
    partial_value = (
        jnp.dot(joined, expert_down, preferred_element_type=jnp.float32)
        .astype(jnp.bfloat16)
        .reshape(2, pairs, EXP, MOST, share_width)
    )
    pair_sum = (
        partial_value[0].astype(jnp.float32)
        + lax.ppermute(partial_value[1], "core", swap).astype(jnp.float32)
    ).astype(jnp.bfloat16)
    outgoing = pair_sum.transpose(1, 0, 2, 3).reshape(EXP * pairs, MOST, share_width)
    returned = lax.all_to_all(outgoing, ("g", "q"), split_axis=0, concat_axis=0, tiled=True)
    summed = jnp.sum(returned.astype(jnp.float32).reshape(EXP, pairs, MOST, share_width), axis=1)
    mixture = jnp.einsum("est,esd->td", weighted, summed, precision=highest)
    return (hidden_share + mixture).astype(jnp.bfloat16)


def solution(mesh):
    ctx_count = mesh.shape["ctx"]
    head_count = mesh.shape["head"]
    split = Mesh(
        mesh.devices.reshape(EXP, ctx_count // EXP // 2, 2, head_count), ("g", "q", "core", "head")
    )
    ctx = CTX
    return jax.shard_map(
        body,
        mesh=split,
        in_specs=(
            P(ctx, "head"),
            P(ctx, "head"),
            P(ctx, "head"),
            P(ctx, "head"),
            P(ctx, "head"),
            P("head"),
            P("head", ctx, None),
            P(ctx, None),
            P(),
            P(),
            P(ctx, None),
            P(ctx + ("head",), None),
            P(ctx + ("head",), None),
            P(ctx, "head"),
        ),
        out_specs=P(ctx, "head"),
        check_vma=False,
    )
```

profile of v0, /device:TPU:34, one launch (start us, length us, event | category | flops | bytes accessed | tf_op | source)
XLA Modules:
  0.0 408.5 jit_solution(14363872480596723360)
XLA Ops:
  16.2 3.8 collective-permute-start.1
  20.0 6.7 %collective-permute-done.1 = f32[4,136,128]{2,1,0:T(8,128)S(1)} collective-permute-done((f32[4,136,128]{2,1,0:T(8,128)S(1)}, f32[4,136,128]{2,1,0:T(8,128)S(1)}, u32[]{:S(2)}, u32[]{:S(2)}) %collective-permute-start.1) | collective-permute-done | bytes 278560 | tf_op jit(solution)/shard_map/ppermute | solution.py:28
  26.9 3.8 collective-permute-start.2
  30.7 8.0 %collective-permute-done.2 = f32[4,136,128]{2,1,0:T(8,128)S(1)} collective-permute-done((f32[4,136,128]{2,1,0:T(8,128)S(1)}, f32[4,136,128]{2,1,0:T(8,128)S(1)}, u32[]{:S(2)}, u32[]{:S(2)}) %collective-permute-start.2) | collective-permute-done | bytes 278560 | tf_op jit(solution)/shard_map/ppermute | solution.py:28
  39.1 8.8 %collective-permute-start.3 = (f32[4,136,128]{2,1,0:T(8,128)S(1)}, f32[4,136,128]{2,1,0:T(8,128)S(1)}, u32[]{:S(2)}, u32[]{:S(2)}) collective-permute-start(f32[4,136,128]{2,1,0:T(8,128)S(1)} %maximum_select_fusion), channel_id=1, source_target_pairs={{0,16},{8,24},{16,32},{24,40},{32,48},{40,56},{48,64},{56,72},{64,... | collective-permute-start | bytes 835592 | tf_op jit(solution)/shard_map/ppermute | solution.py:28
  47.9 10.5 %collective-permute-done.3 = f32[4,136,128]{2,1,0:T(8,128)S(1)} collective-permute-done((f32[4,136,128]{2,1,0:T(8,128)S(1)}, f32[4,136,128]{2,1,0:T(8,128)S(1)}, u32[]{:S(2)}, u32[]{:S(2)}) %collective-permute-start.3) | collective-permute-done | bytes 278560 | tf_op jit(solution)/shard_map/ppermute | solution.py:28
  58.7 7.3 %collective-permute-start.4 = (f32[4,136,128]{2,1,0:T(8,128)S(1)}, f32[4,136,128]{2,1,0:T(8,128)S(1)}, u32[]{:S(2)}, u32[]{:S(2)}) collective-permute-start(f32[4,136,128]{2,1,0:T(8,128)S(1)} %maximum_select_fusion.1), channel_id=1, source_target_pairs={{0,32},{8,40},{16,48},{24,56},{32,64},{40,72},{48,80},{56,88},{64,... | collective-permute-start | bytes 835592 | tf_op jit(solution)/shard_map/ppermute | solution.py:28
  66.1 15.8 %collective-permute-done.4 = f32[4,136,128]{2,1,0:T(8,128)S(1)} collective-permute-done((f32[4,136,128]{2,1,0:T(8,128)S(1)}, f32[4,136,128]{2,1,0:T(8,128)S(1)}, u32[]{:S(2)}, u32[]{:S(2)}) %collective-permute-start.4) | collective-permute-done | bytes 278560 | tf_op jit(solution)/shard_map/ppermute | solution.py:28
  82.2 6.3 %collective-permute-start.5 = (f32[4,136,128]{2,1,0:T(8,128)S(1)}, f32[4,136,128]{2,1,0:T(8,128)S(1)}, u32[]{:S(2)}, u32[]{:S(2)}) collective-permute-start(f32[4,136,128]{2,1,0:T(8,128)S(1)} %maximum_select_fusion.2), channel_id=1, source_target_pairs={{0,64},{8,72},{16,80},{24,88},{32,96},{40,104},{48,112},{56,120},{... | collective-permute-start | bytes 835592 | tf_op jit(solution)/shard_map/ppermute | solution.py:28
  88.5 12.4 %collective-permute-done.5 = f32[4,136,128]{2,1,0:T(8,128)S(1)} collective-permute-done((f32[4,136,128]{2,1,0:T(8,128)S(1)}, f32[4,136,128]{2,1,0:T(8,128)S(1)}, u32[]{:S(2)}, u32[]{:S(2)}) %collective-permute-start.5) | collective-permute-done | bytes 278560 | tf_op jit(solution)/shard_map/ppermute | solution.py:28
  101.3 3.5 collective-permute-start.6
  105.8 3.8 collective-permute-done.6
  119.8 18.2 %bitcast_convert_fusion = bf16[256,4,768]{2,0,1:T(8,128)(2,1)} fusion(bf16[8,128,4,768]{3,0,2,1:T(8,128)(2,1)} %all-gather.4.cloned.1.call-done, bf16[128,8,128]{2,0,1:T(8,128)(2,1)S(1)} %get-tuple-element.25, bf16[128,8,128]{2,0,1:T(8,128)(2,1)S(1)} %get-tuple-element.24), kind=kOutput, calls=%fused_computation.4 | convolution fusion | flops 1612447744 | bytes 8388608 | tf_op jit(solution)/shard_map/thr,hrqd->tqd/dot_general | solution.py:141
  140.5 31.0 %reduce-scatter.2.cloned.1.call-done = bf16[256,1,768]{2,0,1:T(8,128)(2,1)} async-done(((bf16[256,4,768]{2,0,1:T(8,128)(2,1)}), bf16[256,1,768]{2,0,1:T(8,128)(2,1)}) %reduce-scatter.2.cloned.1.call-update) | async-done | bytes 393232 | tf_op jit(solution)/shard_map/reduce_scatter | solution.py:144
  178.1 14.8 %psum.7 = f32[128,33]{0,1:T(8,128)S(1)} all-reduce(f32[128,33]{0,1:T(8,128)S(1)} %pad_maximum_fusion.8), channel_id=1, replica_groups=mesh['g'=8,'q'=4,'core'=2,'head'=4] {'head'}, use_global_device_ids=true, to_apply=%region_7.8 | all-reduce | flops 4224 | bytes 33792 | tf_op jit(solution)/shard_map/psum | solution.py:162
  195.8 22.9 %all_to_all.10 = bf16[8,10,1536]{2,1,0:T(8,128)(2,1)} all-to-all(bf16[8,10,1536]{2,1,0:T(8,128)(2,1)} %reshape.208), channel_id=1, replica_groups=mesh['g'=8,'q'=4,'core'=2,'head'=4] {'g'}, dimensions={0} | all-to-all | bytes 491520 | tf_op jit(solution)/shard_map/all_to_all | solution.py:195
  220.5 16.9 %all_gather.16 = bf16[80,6144]{1,0:T(8,128)(2,1)} all-gather(bf16[80,1536]{1,0:T(8,128)(2,1)} %reshape.209), channel_id=1, replica_groups=mesh['g'=8,'q'=4,'core'=2,'head'=4] {'head'}, dimensions={1}, use_global_device_ids=true | all-gather | bytes 1228800 | tf_op jit(solution)/shard_map/all_gather | solution.py:196
  237.4 74.8 %all-gather.6.cloned.1.call-done = bf16[320,6144]{1,0:T(8,128)(2,1)} async-done(((bf16[80,6144]{1,0:T(8,128)(2,1)}), bf16[320,6144]{1,0:T(8,128)(2,1)}) %all-gather.6.cloned.1.call-update) | async-done | bytes 3932176 | tf_op jit(solution)/shard_map/all_gather | solution.py:197
  312.2 3.8 fusion.76
  322.6 14.0 %all_gather.19 = bf16[640,576]{0,1:T(8,128)(2,1)S(1)} all-gather(bf16[640,144]{0,1:T(8,128)(2,1)S(1)} %pad_maximum_fusion.7), channel_id=1, replica_groups=mesh['g'=8,'q'=4,'core'=2,'head'=4] {'head'}, dimensions={1}, use_global_device_ids=true | all-gather | bytes 921600 | tf_op jit(solution)/shard_map/all_gather | solution.py:209
  343.0 3.0 reshape.215
  346.0 2.5 fusion.6
  348.6 49.5 %all_to_all.11 = bf16[32,10,1536]{2,1,0:T(8,128)(2,1)S(1)} all-to-all(bf16[32,10,1536]{2,1,0:T(8,128)(2,1)S(1)} %bitcast.105), channel_id=1, replica_groups=mesh['g'=8,'q'=4,'core'=2,'head'=4] {'g','q'}, dimensions={0} | all-to-all | bytes 1966080 | tf_op jit(solution)/shard_map/all_to_all | solution.py:220
  399.1 2.8 fusion.3
  (158 shorter events, 49.8 us)
Async XLA Ops:
  6.5 330.0 %copy-start = (bf16[576,1536]{1,0:T(8,128)(2,1)S(1)}, bf16[576,1536]{1,0:T(8,128)(2,1)}, u32[]{:S(2)}) copy-start(bf16[576,1536]{1,0:T(8,128)(2,1)} %param.27) | copy-start | bytes 5308420
  6.5 113.3 %all-gather.4.cloned.1.call-start = ((), (), s32[]{:S(2)}) async-start(), calls=%async_computation.3 | async-start | bytes 6488064 | tf_op jit(solution)/shard_map/all_gather | solution.py:132
  8.5 1.4 collective-permute-start.9
  10.6 160.8 %reduce-scatter.2.cloned.1.call-start = ((), (), s32[]{:S(2)}) async-start(), calls=%async_computation.4 | async-start | bytes 1966080 | tf_op jit(solution)/shard_map/reduce_scatter | solution.py:144
  13.5 2.2 collective-permute-start
  15.6 23.2 %copy-start.3 = (f32[8,136,128]{2,1,0:T(8,128)}, f32[8,136,128]{2,1,0:T(8,128)S(1)}, u32[]{:S(2)}) copy-start(f32[8,136,128]{2,1,0:T(8,128)S(1)} %collective-permute-done) | copy-start | bytes 1671172
  16.2 10.6 %collective-permute-start.1 = (f32[4,136,128]{2,1,0:T(8,128)S(1)}, f32[4,136,128]{2,1,0:T(8,128)S(1)}, u32[]{:S(2)}, u32[]{:S(2)}) collective-permute-start(f32[4,136,128]{2,1,0:T(8,128)S(1)} %pad_maximum_fusion.4), channel_id=1, source_target_pairs={{0,8},{8,16},{16,24},{24,32},{32,40},{40,48},{48,56},{56,64},{64,7... | collective-permute-start | bytes 835592 | tf_op jit(solution)/shard_map/ppermute | solution.py:28
  26.9 11.8 %collective-permute-start.2 = (f32[4,136,128]{2,1,0:T(8,128)S(1)}, f32[4,136,128]{2,1,0:T(8,128)S(1)}, u32[]{:S(2)}, u32[]{:S(2)}) collective-permute-start(f32[4,136,128]{2,1,0:T(8,128)S(1)} %broadcast_select_fusion.5), channel_id=1, source_target_pairs={{0,8},{8,16},{16,24},{24,32},{32,40},{40,48},{48,56},{56,64},{64,7... | collective-permute-start | bytes 835592 | tf_op jit(solution)/shard_map/ppermute | solution.py:28
  39.1 19.3 %collective-permute-start.3 = (f32[4,136,128]{2,1,0:T(8,128)S(1)}, f32[4,136,128]{2,1,0:T(8,128)S(1)}, u32[]{:S(2)}, u32[]{:S(2)}) collective-permute-start(f32[4,136,128]{2,1,0:T(8,128)S(1)} %maximum_select_fusion), channel_id=1, source_target_pairs={{0,16},{8,24},{16,32},{24,40},{32,48},{40,56},{48,64},{56,72},{64,... | collective-permute-start | bytes 835592 | tf_op jit(solution)/shard_map/ppermute | solution.py:28
  58.7 46.2 %copy-start.13 = (bf16[128,1024]{1,0:T(8,128)(2,1)S(1)}, bf16[128,1024]{1,0:T(8,128)(2,1)}, u32[]{:S(2)}) copy-start(bf16[128,1024]{1,0:T(8,128)(2,1)} %param.17) | copy-start | bytes 786436
  58.7 23.1 %collective-permute-start.4 = (f32[4,136,128]{2,1,0:T(8,128)S(1)}, f32[4,136,128]{2,1,0:T(8,128)S(1)}, u32[]{:S(2)}, u32[]{:S(2)}) collective-permute-start(f32[4,136,128]{2,1,0:T(8,128)S(1)} %maximum_select_fusion.1), channel_id=1, source_target_pairs={{0,32},{8,40},{16,48},{24,56},{32,64},{40,72},{48,80},{56,88},{64,... | collective-permute-start | bytes 835592 | tf_op jit(solution)/shard_map/ppermute | solution.py:28
  82.2 18.7 %collective-permute-start.5 = (f32[4,136,128]{2,1,0:T(8,128)S(1)}, f32[4,136,128]{2,1,0:T(8,128)S(1)}, u32[]{:S(2)}, u32[]{:S(2)}) collective-permute-start(f32[4,136,128]{2,1,0:T(8,128)S(1)} %maximum_select_fusion.2), channel_id=1, source_target_pairs={{0,64},{8,72},{16,80},{24,88},{32,96},{40,104},{48,112},{56,120},{... | collective-permute-start | bytes 835592 | tf_op jit(solution)/shard_map/ppermute | solution.py:28
  101.3 8.3 %collective-permute-start.6 = (f32[4,136,128]{2,1,0:T(8,128)S(1)}, f32[4,136,128]{2,1,0:T(8,128)S(1)}, u32[]{:S(2)}, u32[]{:S(2)}) collective-permute-start(f32[4,136,128]{2,1,0:T(8,128)S(1)} %maximum_select_fusion.3), channel_id=1, source_target_pairs={{0,128},{8,136},{16,144},{24,152},{32,160},{40,168},{48,176},{56,1... | collective-permute-start | bytes 835592 | tf_op jit(solution)/shard_map/ppermute | solution.py:28
  110.6 1.9 collective-permute-start.7
  111.0 5.1 %copy-start.10 = (bf16[128,1024]{0,1:T(8,128)(2,1)S(1)}, bf16[128,1024]{0,1:T(8,128)(2,1)}, u32[]{:S(2)}) copy-start(bf16[128,1024]{0,1:T(8,128)(2,1)} %copy-done.9) | copy-start | bytes 786436
  117.9 1.8 collective-permute-start.8
  119.8 18.3 %copy-start.15 = (s32[128,2]{0,1:T(2,128)S(1)}, s32[128,2]{0,1:T(2,128)}, u32[]{:S(2)}) copy-start(s32[128,2]{0,1:T(2,128)} %param.24) | copy-start | bytes 3076
  138.0 174.2 %all-gather.6.cloned.1.call-start = ((), (), s32[]{:S(2)}) async-start(), calls=%async_computation.5 | async-start | bytes 4915200 | tf_op jit(solution)/shard_map/all_gather | solution.py:197
  172.5 1.5 collective-permute-start.10
  175.1 19.9 %copy-start.4 = (bf16[128,768]{1,0:T(8,128)(2,1)}, bf16[128,768]{1,0:T(8,128)(2,1)S(1)}, u32[]{:S(2)}) copy-start(bf16[128,768]{1,0:T(8,128)(2,1)S(1)} %get-tuple-element.22) | copy-start | bytes 589828
  175.1 19.9 %copy-start.6 = (bf16[128,768]{1,0:T(8,128)(2,1)}, bf16[128,768]{1,0:T(8,128)(2,1)S(1)}, u32[]{:S(2)}) copy-start(bf16[128,768]{1,0:T(8,128)(2,1)S(1)} %get-tuple-element.23) | copy-start | bytes 589828
  195.8 116.4 %copy-start.1 = (bf16[144,6144]{1,0:T(8,128)(2,1)S(1)}, bf16[144,6144]{1,0:T(8,128)(2,1)}, u32[]{:S(2)}) copy-start(bf16[144,6144]{1,0:T(8,128)(2,1)} %param.25) | copy-start | bytes 5308420
  312.2 7.0 %collective-permute-start.11 = (bf16[4,80,6144]{2,1,0:T(8,128)(2,1)}, bf16[4,80,6144]{2,1,0:T(8,128)(2,1)S(1)}, u32[]{:S(2)}, u32[]{:S(2)}) collective-permute-start(bf16[4,80,6144]{2,1,0:T(8,128)(2,1)} %bitcast.106), channel_id=1, source_target_pairs={{0,4},{4,0},{1,5},{5,1},{2,6},{6,2},{3,7},{7,3},{8,12},{12,8},{9,1... | collective-permute-start | bytes 11796488 | tf_op jit(solution)/shard_map/ppermute | solution.py:198
  343.0 3.0 collective-permute-start.12
  (11 other events, 33.5 us)
Sparse Core Ops, SparseCore 0:
  10.8 99.6 all-gather.3
  138.2 33.2 reduce-scatter.1
  237.5 74.6 all-gather.5
where the time goes:
time: 409 us; the launch traced here: 408 us
  waiting for transfers between devices  172 us (42%)
  blocking collectives  118 us (29%)
  matrix products  39.7 us (10%)
  starting transfers between devices  34.5 us (8%)
  other arithmetic  15.7 us (4%)
  local copies, waits for them, and re-layouts  14.7 us (4%)
  between operations  13.7 us (3%)
    all_gather x1, waiting for transfers between devices, body(): own_parity = lax.all_gather(wide, 'q', axis=0, tiled=False)  74.8 us
    ppermute x6, waiting for transfers between devices, shift(): lax.ppermute(value, axis, [(i, i + distance) for i in range(count - dista...  57.2 us
    all_to_all x1, blocking collectives, body(): lax.all_to_all(outgoing, ('g', 'q'), split_axis=0, concat_axis=0, tiled=T...  49.5 us
    ppermute x6, starting transfers between devices, shift(): lax.ppermute(value, axis, [(i, i + distance) for i in range(count - dista...  33.6 us
    reduce_scatter x1, waiting for transfers between devices, body(): lax.psum_scatter(partial_sum.astype(jnp.bfloat16), 'head', scatter_dimens...  31 us
    all_to_all x1, blocking collectives, body(): lax.all_to_all(packed, 'g', split_axis=0, concat_axis=0, tiled=True)  22.9 us
    dot_general x1, matrix products, body(): jnp.einsum('thr,hrqd->tqd', both_mixed, row_whole, preferred_element_type...  18.2 us
    all_gather x1, blocking collectives, body(): lax.all_gather(by_group.reshape(EXP * MOST, share_width), 'head', axis=1,...  16.9 us
  transfers between devices with their start and end apart: 16, of which 14 were waited for; matrix products, arithmetic and copies ran while one was open for 6% of the time, Pallas kernels for 0%

commit v1 on v0

--- a/solution.py
+++ b/solution.py
@@ -159,7 +159,9 @@
         hidden_share * gain_share[None, :], router_share.astype(jnp.float32), precision=highest
     )
     square_part = jnp.sum(hidden_share * hidden_share, axis=-1, keepdims=True)
-    stats = lax.psum(jnp.concatenate([square_part, router_part], axis=1), "head")
+    stats = lax.all_gather(
+        jnp.concatenate([square_part, router_part], axis=1), axis_name="head"
+    ).sum(axis=0)
     row_scale = lax.rsqrt(stats[:, :1] / model_width + epsilon)
     logits = stats[:, 1:] * row_scale
     normed_share = (hidden_share * row_scale * gain_share[None, :]).astype(jnp.bfloat16)

time: 409 us -> 405 us (level)
  blocking collectives: 118 us -> 113 us
    psum x1 -> x0, blocking collectives: 14.8 us -> none  [body(): lax.psum(jnp.concatenate([square_part, router_part], axis=1), 'head')]
    all_gather x0 -> x1, blocking collectives: none -> 11.9 us  [body(): lax.all_gather(jnp.concatenate([square_part, router_part], axis=1), axis_...]
where the time goes in v1:
time: 405 us; the launch traced here: 404 us
  waiting for transfers between devices  172 us (42%)
  blocking collectives  113 us (28%)
  matrix products  39.7 us (10%)
  starting transfers between devices  34.5 us (9%)
  other arithmetic  15.7 us (4%)
  local copies, waits for them, and re-layouts  14.8 us (4%)
  between operations  13.7 us (3%)
    all_gather x1, waiting for transfers between devices, body(): own_parity = lax.all_gather(wide, 'q', axis=0, tiled=False)  75 us
    ppermute x6, waiting for transfers between devices, shift(): lax.ppermute(value, axis, [(i, i + distance) for i in range(count - dista...  57.2 us
    all_to_all x1, blocking collectives, body(): lax.all_to_all(outgoing, ('g', 'q'), split_axis=0, concat_axis=0, tiled=T...  49.5 us
    ppermute x6, starting transfers between devices, shift(): lax.ppermute(value, axis, [(i, i + distance) for i in range(count - dista...  33.6 us
    reduce_scatter x1, waiting for transfers between devices, body(): lax.psum_scatter(partial_sum.astype(jnp.bfloat16), 'head', scatter_dimens...  31 us
    all_to_all x1, blocking collectives, body(): lax.all_to_all(packed, 'g', split_axis=0, concat_axis=0, tiled=True)  23.1 us
    dot_general x1, matrix products, body(): jnp.einsum('thr,hrqd->tqd', both_mixed, row_whole, preferred_element_type...  18.2 us
    all_gather x1, blocking collectives, body(): lax.all_gather(by_group.reshape(EXP * MOST, share_width), 'head', axis=1,...  14.8 us
  transfers between devices with their start and end apart: 16, of which 14 were waited for; matrix products, arithmetic and copies ran while one was open for 6% of the time, Pallas kernels for 0%

profile of v1, /device:TPU:34, one launch (start us, length us, event | category | flops | bytes accessed | tf_op | source)
XLA Modules:
  0.0 404.0 jit_solution(5165751578406027457)
XLA Ops:
  16.2 3.8 collective-permute-start.1
  20.0 6.7 %collective-permute-done.1 = f32[4,136,128]{2,1,0:T(8,128)S(1)} collective-permute-done((f32[4,136,128]{2,1,0:T(8,128)S(1)}, f32[4,136,128]{2,1,0:T(8,128)S(1)}, u32[]{:S(2)}, u32[]{:S(2)}) %collective-permute-start.1) | collective-permute-done | bytes 278560 | tf_op jit(solution)/shard_map/ppermute | solution.py:28
  26.9 3.8 collective-permute-start.2
  30.7 8.0 %collective-permute-done.2 = f32[4,136,128]{2,1,0:T(8,128)S(1)} collective-permute-done((f32[4,136,128]{2,1,0:T(8,128)S(1)}, f32[4,136,128]{2,1,0:T(8,128)S(1)}, u32[]{:S(2)}, u32[]{:S(2)}) %collective-permute-start.2) | collective-permute-done | bytes 278560 | tf_op jit(solution)/shard_map/ppermute | solution.py:28
  39.1 8.8 %collective-permute-start.3 = (f32[4,136,128]{2,1,0:T(8,128)S(1)}, f32[4,136,128]{2,1,0:T(8,128)S(1)}, u32[]{:S(2)}, u32[]{:S(2)}) collective-permute-start(f32[4,136,128]{2,1,0:T(8,128)S(1)} %maximum_select_fusion), channel_id=1, source_target_pairs={{0,16},{8,24},{16,32},{24,40},{32,48},{40,56},{48,64},{56,72},{64,... | collective-permute-start | bytes 835592 | tf_op jit(solution)/shard_map/ppermute | solution.py:28
  47.9 10.5 %collective-permute-done.3 = f32[4,136,128]{2,1,0:T(8,128)S(1)} collective-permute-done((f32[4,136,128]{2,1,0:T(8,128)S(1)}, f32[4,136,128]{2,1,0:T(8,128)S(1)}, u32[]{:S(2)}, u32[]{:S(2)}) %collective-permute-start.3) | collective-permute-done | bytes 278560 | tf_op jit(solution)/shard_map/ppermute | solution.py:28
  58.7 7.3 %collective-permute-start.4 = (f32[4,136,128]{2,1,0:T(8,128)S(1)}, f32[4,136,128]{2,1,0:T(8,128)S(1)}, u32[]{:S(2)}, u32[]{:S(2)}) collective-permute-start(f32[4,136,128]{2,1,0:T(8,128)S(1)} %maximum_select_fusion.1), channel_id=1, source_target_pairs={{0,32},{8,40},{16,48},{24,56},{32,64},{40,72},{48,80},{56,88},{64,... | collective-permute-start | bytes 835592 | tf_op jit(solution)/shard_map/ppermute | solution.py:28
  66.1 15.8 %collective-permute-done.4 = f32[4,136,128]{2,1,0:T(8,128)S(1)} collective-permute-done((f32[4,136,128]{2,1,0:T(8,128)S(1)}, f32[4,136,128]{2,1,0:T(8,128)S(1)}, u32[]{:S(2)}, u32[]{:S(2)}) %collective-permute-start.4) | collective-permute-done | bytes 278560 | tf_op jit(solution)/shard_map/ppermute | solution.py:28
  82.2 6.3 %collective-permute-start.5 = (f32[4,136,128]{2,1,0:T(8,128)S(1)}, f32[4,136,128]{2,1,0:T(8,128)S(1)}, u32[]{:S(2)}, u32[]{:S(2)}) collective-permute-start(f32[4,136,128]{2,1,0:T(8,128)S(1)} %maximum_select_fusion.2), channel_id=1, source_target_pairs={{0,64},{8,72},{16,80},{24,88},{32,96},{40,104},{48,112},{56,120},{... | collective-permute-start | bytes 835592 | tf_op jit(solution)/shard_map/ppermute | solution.py:28
  88.5 12.4 %collective-permute-done.5 = f32[4,136,128]{2,1,0:T(8,128)S(1)} collective-permute-done((f32[4,136,128]{2,1,0:T(8,128)S(1)}, f32[4,136,128]{2,1,0:T(8,128)S(1)}, u32[]{:S(2)}, u32[]{:S(2)}) %collective-permute-start.5) | collective-permute-done | bytes 278560 | tf_op jit(solution)/shard_map/ppermute | solution.py:28
  101.3 3.5 collective-permute-start.6
  105.8 3.8 collective-permute-done.6
  119.8 18.2 %bitcast_convert_fusion = bf16[256,4,768]{2,0,1:T(8,128)(2,1)} fusion(bf16[8,128,4,768]{3,0,2,1:T(8,128)(2,1)} %all-gather.5.cloned.1.call-done, bf16[128,8,128]{2,0,1:T(8,128)(2,1)S(1)} %get-tuple-element.25, bf16[128,8,128]{2,0,1:T(8,128)(2,1)S(1)} %get-tuple-element.24), kind=kOutput, calls=%fused_computation.4 | convolution fusion | flops 1612447744 | bytes 8388608 | tf_op jit(solution)/shard_map/thr,hrqd->tqd/dot_general | solution.py:141
  140.5 31.0 %reduce-scatter.2.cloned.1.call-done = bf16[256,1,768]{2,0,1:T(8,128)(2,1)} async-done(((bf16[256,4,768]{2,0,1:T(8,128)(2,1)}), bf16[256,1,768]{2,0,1:T(8,128)(2,1)}) %reduce-scatter.2.cloned.1.call-update) | async-done | bytes 393232 | tf_op jit(solution)/shard_map/reduce_scatter | solution.py:144
  178.1 11.9 %all-gather = f32[512,33]{0,1:T(8,128)S(1)} all-gather(f32[128,33]{0,1:T(8,128)S(1)} %pad_maximum_fusion.8), channel_id=2, replica_groups=mesh['g'=8,'q'=4,'core'=2,'head'=4] {'head'}, dimensions={0}, use_global_device_ids=true | all-gather | bytes 84480 | tf_op jit(solution)/shard_map/all_gather | solution.py:162
  193.0 23.1 %all_to_all.10 = bf16[8,10,1536]{2,1,0:T(8,128)(2,1)} all-to-all(bf16[8,10,1536]{2,1,0:T(8,128)(2,1)} %reshape.208), channel_id=1, replica_groups=mesh['g'=8,'q'=4,'core'=2,'head'=4] {'g'}, dimensions={0} | all-to-all | bytes 491520 | tf_op jit(solution)/shard_map/all_to_all | solution.py:197
  217.9 14.8 %all_gather.24 = bf16[80,6144]{1,0:T(8,128)(2,1)} all-gather(bf16[80,1536]{1,0:T(8,128)(2,1)} %reshape.209), channel_id=1, replica_groups=mesh['g'=8,'q'=4,'core'=2,'head'=4] {'head'}, dimensions={1}, use_global_device_ids=true | all-gather | bytes 1228800 | tf_op jit(solution)/shard_map/all_gather | solution.py:198
  232.8 75.0 %all-gather.7.cloned.1.call-done = bf16[320,6144]{1,0:T(8,128)(2,1)} async-done(((bf16[80,6144]{1,0:T(8,128)(2,1)}), bf16[320,6144]{1,0:T(8,128)(2,1)}) %all-gather.7.cloned.1.call-update) | async-done | bytes 3932176 | tf_op jit(solution)/shard_map/all_gather | solution.py:199
  307.7 3.8 fusion.76
  318.1 14.0 %all_gather.27 = bf16[640,576]{0,1:T(8,128)(2,1)S(1)} all-gather(bf16[640,144]{0,1:T(8,128)(2,1)S(1)} %pad_maximum_fusion.7), channel_id=1, replica_groups=mesh['g'=8,'q'=4,'core'=2,'head'=4] {'head'}, dimensions={1}, use_global_device_ids=true | all-gather | bytes 921600 | tf_op jit(solution)/shard_map/all_gather | solution.py:211
  338.5 3.0 reshape.215
  341.5 2.5 fusion.6
  344.1 49.5 %all_to_all.11 = bf16[32,10,1536]{2,1,0:T(8,128)(2,1)S(1)} all-to-all(bf16[32,10,1536]{2,1,0:T(8,128)(2,1)S(1)} %bitcast.107), channel_id=1, replica_groups=mesh['g'=8,'q'=4,'core'=2,'head'=4] {'g','q'}, dimensions={0} | all-to-all | bytes 1966080 | tf_op jit(solution)/shard_map/all_to_all | solution.py:222
  394.7 2.8 fusion.3
  (160 shorter events, 49.8 us)
Async XLA Ops:
  6.5 325.6 %copy-start = (bf16[576,1536]{1,0:T(8,128)(2,1)S(1)}, bf16[576,1536]{1,0:T(8,128)(2,1)}, u32[]{:S(2)}) copy-start(bf16[576,1536]{1,0:T(8,128)(2,1)} %param.27) | copy-start | bytes 5308420
  6.5 113.3 %all-gather.5.cloned.1.call-start = ((), (), s32[]{:S(2)}) async-start(), calls=%async_computation.3 | async-start | bytes 6488064 | tf_op jit(solution)/shard_map/all_gather | solution.py:132
  8.5 1.4 collective-permute-start.9
  10.6 160.8 %reduce-scatter.2.cloned.1.call-start = ((), (), s32[]{:S(2)}) async-start(), calls=%async_computation.4 | async-start | bytes 1966080 | tf_op jit(solution)/shard_map/reduce_scatter | solution.py:144
  13.5 2.2 collective-permute-start
  15.6 23.2 %copy-start.3 = (f32[8,136,128]{2,1,0:T(8,128)}, f32[8,136,128]{2,1,0:T(8,128)S(1)}, u32[]{:S(2)}) copy-start(f32[8,136,128]{2,1,0:T(8,128)S(1)} %collective-permute-done) | copy-start | bytes 1671172
  16.2 10.6 %collective-permute-start.1 = (f32[4,136,128]{2,1,0:T(8,128)S(1)}, f32[4,136,128]{2,1,0:T(8,128)S(1)}, u32[]{:S(2)}, u32[]{:S(2)}) collective-permute-start(f32[4,136,128]{2,1,0:T(8,128)S(1)} %pad_maximum_fusion.4), channel_id=1, source_target_pairs={{0,8},{8,16},{16,24},{24,32},{32,40},{40,48},{48,56},{56,64},{64,7... | collective-permute-start | bytes 835592 | tf_op jit(solution)/shard_map/ppermute | solution.py:28
  26.9 11.8 %collective-permute-start.2 = (f32[4,136,128]{2,1,0:T(8,128)S(1)}, f32[4,136,128]{2,1,0:T(8,128)S(1)}, u32[]{:S(2)}, u32[]{:S(2)}) collective-permute-start(f32[4,136,128]{2,1,0:T(8,128)S(1)} %broadcast_select_fusion.5), channel_id=1, source_target_pairs={{0,8},{8,16},{16,24},{24,32},{32,40},{40,48},{48,56},{56,64},{64,7... | collective-permute-start | bytes 835592 | tf_op jit(solution)/shard_map/ppermute | solution.py:28
  39.1 19.3 %collective-permute-start.3 = (f32[4,136,128]{2,1,0:T(8,128)S(1)}, f32[4,136,128]{2,1,0:T(8,128)S(1)}, u32[]{:S(2)}, u32[]{:S(2)}) collective-permute-start(f32[4,136,128]{2,1,0:T(8,128)S(1)} %maximum_select_fusion), channel_id=1, source_target_pairs={{0,16},{8,24},{16,32},{24,40},{32,48},{40,56},{48,64},{56,72},{64,... | collective-permute-start | bytes 835592 | tf_op jit(solution)/shard_map/ppermute | solution.py:28
  58.7 46.2 %copy-start.13 = (bf16[128,1024]{1,0:T(8,128)(2,1)S(1)}, bf16[128,1024]{1,0:T(8,128)(2,1)}, u32[]{:S(2)}) copy-start(bf16[128,1024]{1,0:T(8,128)(2,1)} %param.17) | copy-start | bytes 786436
  58.7 23.1 %collective-permute-start.4 = (f32[4,136,128]{2,1,0:T(8,128)S(1)}, f32[4,136,128]{2,1,0:T(8,128)S(1)}, u32[]{:S(2)}, u32[]{:S(2)}) collective-permute-start(f32[4,136,128]{2,1,0:T(8,128)S(1)} %maximum_select_fusion.1), channel_id=1, source_target_pairs={{0,32},{8,40},{16,48},{24,56},{32,64},{40,72},{48,80},{56,88},{64,... | collective-permute-start | bytes 835592 | tf_op jit(solution)/shard_map/ppermute | solution.py:28
  82.2 18.7 %collective-permute-start.5 = (f32[4,136,128]{2,1,0:T(8,128)S(1)}, f32[4,136,128]{2,1,0:T(8,128)S(1)}, u32[]{:S(2)}, u32[]{:S(2)}) collective-permute-start(f32[4,136,128]{2,1,0:T(8,128)S(1)} %maximum_select_fusion.2), channel_id=1, source_target_pairs={{0,64},{8,72},{16,80},{24,88},{32,96},{40,104},{48,112},{56,120},{... | collective-permute-start | bytes 835592 | tf_op jit(solution)/shard_map/ppermute | solution.py:28
  101.3 8.3 %collective-permute-start.6 = (f32[4,136,128]{2,1,0:T(8,128)S(1)}, f32[4,136,128]{2,1,0:T(8,128)S(1)}, u32[]{:S(2)}, u32[]{:S(2)}) collective-permute-start(f32[4,136,128]{2,1,0:T(8,128)S(1)} %maximum_select_fusion.3), channel_id=1, source_target_pairs={{0,128},{8,136},{16,144},{24,152},{32,160},{40,168},{48,176},{56,1... | collective-permute-start | bytes 835592 | tf_op jit(solution)/shard_map/ppermute | solution.py:28
  110.6 1.9 collective-permute-start.7
  111.0 5.1 %copy-start.10 = (bf16[128,1024]{0,1:T(8,128)(2,1)S(1)}, bf16[128,1024]{0,1:T(8,128)(2,1)}, u32[]{:S(2)}) copy-start(bf16[128,1024]{0,1:T(8,128)(2,1)} %copy-done.9) | copy-start | bytes 786436
  117.9 1.8 collective-permute-start.8
  119.8 18.3 %copy-start.15 = (s32[128,2]{0,1:T(2,128)S(1)}, s32[128,2]{0,1:T(2,128)}, u32[]{:S(2)}) copy-start(s32[128,2]{0,1:T(2,128)} %param.24) | copy-start | bytes 3076
  138.0 169.7 %all-gather.7.cloned.1.call-start = ((), (), s32[]{:S(2)}) async-start(), calls=%async_computation.5 | async-start | bytes 4915200 | tf_op jit(solution)/shard_map/all_gather | solution.py:199
  172.5 1.5 collective-permute-start.10
  175.1 17.1 %copy-start.4 = (bf16[128,768]{1,0:T(8,128)(2,1)}, bf16[128,768]{1,0:T(8,128)(2,1)S(1)}, u32[]{:S(2)}) copy-start(bf16[128,768]{1,0:T(8,128)(2,1)S(1)} %get-tuple-element.22) | copy-start | bytes 589828
  175.1 17.1 %copy-start.6 = (bf16[128,768]{1,0:T(8,128)(2,1)}, bf16[128,768]{1,0:T(8,128)(2,1)S(1)}, u32[]{:S(2)}) copy-start(bf16[128,768]{1,0:T(8,128)(2,1)S(1)} %get-tuple-element.23) | copy-start | bytes 589828
  193.0 114.7 %copy-start.1 = (bf16[144,6144]{1,0:T(8,128)(2,1)S(1)}, bf16[144,6144]{1,0:T(8,128)(2,1)}, u32[]{:S(2)}) copy-start(bf16[144,6144]{1,0:T(8,128)(2,1)} %param.25) | copy-start | bytes 5308420
  307.7 7.0 %collective-permute-start.11 = (bf16[4,80,6144]{2,1,0:T(8,128)(2,1)}, bf16[4,80,6144]{2,1,0:T(8,128)(2,1)S(1)}, u32[]{:S(2)}, u32[]{:S(2)}) collective-permute-start(bf16[4,80,6144]{2,1,0:T(8,128)(2,1)} %bitcast.108), channel_id=1, source_target_pairs={{0,4},{4,0},{1,5},{5,1},{2,6},{6,2},{3,7},{7,3},{8,12},{12,8},{9,1... | collective-permute-start | bytes 11796488 | tf_op jit(solution)/shard_map/ppermute | solution.py:200
  338.5 3.0 collective-permute-start.12
  (11 other events, 33.5 us)
Sparse Core Ops, SparseCore 0:
  10.8 99.6 all-gather.4
  138.2 33.2 reduce-scatter.1
  232.9 74.7 all-gather.6
